TPU v7x, 256 devices: a whole 4x4x8 slice. The times are simulated.
256 devices in a mesh: section: 16 (over x, z_lo, core), dp: 16 (over z_hi, y).
Axes of the slice: x: 4, y: 4, z: 8 (z_hi: 4, z_lo: 2; z = z_hi * 2 + z_lo), core: 2. Of those that a mesh axis runs over, the one named last changes fastest.
Arguments:
- encoder_out: bfloat16 [2, 2, 256, 4096], P(None, None, 'dp', 'section'), may hold values from -6 to 6
- encoder_len: int32 [2, 2], replicated, may hold values from 1 to 2, as said below
- decoder_len: int32 [2, 2], replicated, may hold values from 1 to 2, as said below
- queries: bfloat16 [16, 2, 2, 256, 4096], P('section', None, None, None, 'dp'), may hold values from -40 to 40
- cotangent: bfloat16 [16, 2, 2, 256, 4096], P('section', None, None, None, 'dp'), may hold values from -6 to 6
- key_weight: bfloat16 [16, 4096, 4096], P('section', None, 'dp'), may hold values from -0.09375 to 0.09375
- value_weight: bfloat16 [16, 4096, 4096], P('section', None, 'dp'), may hold values from -0.09375 to 0.09375
Outputs:
- attention: bfloat16 [16, 2, 2, 256, 4096], P('section', None, None, None, 'dp')
- grad_query: bfloat16 [16, 2, 2, 256, 4096], P('section', None, None, None, 'dp')
- grad_key_weight: bfloat16 [16, 4096, 4096], P('section', None, 'dp')
- grad_value_weight: bfloat16 [16, 4096, 4096], P('section', None, 'dp')
- grad_encoder: float32 [2, 2, 256, 4096], P(None, None, 'dp', 'section')
Inputs may be any that keep to these rules, and one draw needn't show every extreme that they name: `encoder_len`: in every micro-batch some example fills all 2 encoder blocks. `decoder_len`: in every micro-batch some example fills all 2 decoder blocks.
All inputs are finite; a program needn't handle non-finite values.
Results may differ from a plain program's by a relative error of at most 0.012.
The roundings to bfloat16 on the way count: a program that leaves them out, or rounds other values in their place, can miss the bound.
Values may be sent and summed in bfloat16 or wider, within the bound.
No kernel may reach another device: no remote copies, remote signals or barrier semaphores. Data moves between devices by JAX's collectives and lax.ppermute only.
A program may use at most 128 MiB of HBM per device.

v0:
```python
import jax
import jax.numpy as jnp
from jax import lax
from jax.sharding import PartitionSpec as P

HD = 256
BLOCK = 128
ENC_BLOCKS = 2
MICRO = 2
NEG_FILL = -1e30


def attend(query_rows, key_rows, value_rows, cotan_rows, key_valid, query_valid):
    score_scale = HD ** (-0.5)
    scores = (
        jnp.einsum("eqhd,ekhd->ehqk", query_rows, key_rows, preferred_element_type=jnp.float32)
        * score_scale
    )
    scores = jnp.where(key_valid[:, None, None, :], scores, NEG_FILL)
    largest = jnp.max(scores, axis=-1, keepdims=True)
    weights = jnp.exp(scores - largest)
    probs = weights / jnp.sum(weights, axis=-1, keepdims=True)
    probs_low = probs.astype(jnp.bfloat16)
    attended = jnp.einsum(
        "ehqk,ekhd->eqhd", probs_low, value_rows, preferred_element_type=jnp.float32
    )
    attended = jnp.where(query_valid[:, :, None, None], attended, 0.0).astype(jnp.bfloat16)
    cotan_kept = jnp.where(query_valid[:, :, None, None], cotan_rows, jnp.zeros_like(cotan_rows))
    grad_value = jnp.einsum(
        "ehqk,eqhd->ekhd", probs_low, cotan_kept, preferred_element_type=jnp.float32
    ).astype(jnp.bfloat16)
    grad_probs = jnp.einsum(
        "eqhd,ekhd->ehqk", cotan_kept, value_rows, preferred_element_type=jnp.float32
    )
    inner_sum = jnp.sum(probs * grad_probs, axis=-1, keepdims=True)
    grad_scores = (probs * (grad_probs - inner_sum) * score_scale).astype(jnp.bfloat16)
    grad_query = jnp.einsum(
        "ehqk,ekhd->eqhd", grad_scores, key_rows, preferred_element_type=jnp.float32
    ).astype(jnp.bfloat16)
    grad_key = jnp.einsum(
        "ehqk,eqhd->ekhd", grad_scores, query_rows, preferred_element_type=jnp.float32
    ).astype(jnp.bfloat16)
    return (attended, grad_query, grad_key, grad_value)


def body(encoder_out, encoder_len, decoder_len, queries, cotangent, key_weight, value_weight):
    key_mat = key_weight[0]
    value_mat = value_weight[0]
    width_dev = key_mat.shape[1]
    heads_dev = width_dev // HD
    enc_rows = ENC_BLOCKS * BLOCK
    dec_rows = queries.shape[3]
    examples = queries.shape[2]
    rows_dev = enc_rows // lax.axis_size("dp")
    key_positions = jnp.arange(enc_rows, dtype=jnp.int32)
    query_positions = jnp.arange(dec_rows, dtype=jnp.int32)
    key_acc = jnp.zeros(key_mat.shape, jnp.float32)
    value_acc = jnp.zeros(value_mat.shape, jnp.float32)
    attn_list, query_list, encoder_list = ([], [], [])
    groups = lax.axis_size("dp")
    copies = jnp.broadcast_to(encoder_out[None], (groups,) + encoder_out.shape)
    from_each = lax.all_to_all(copies, "dp", 0, 0, tiled=True)
    tall_enc = jnp.moveaxis(from_each, 0, 2).reshape(
        encoder_out.shape[:2] + (groups * encoder_out.shape[2], encoder_out.shape[3])
    )
    gathered_enc = lax.all_gather(tall_enc, "section", axis=3, tiled=True)
    for micro_idx in range(MICRO):
        whole_enc = gathered_enc[micro_idx]
        key_rows = jnp.einsum(
            "ekd,dc->ekc", whole_enc, key_mat, preferred_element_type=jnp.float32
        ).astype(jnp.bfloat16)
        value_rows = jnp.einsum(
            "ekd,dc->ekc", whole_enc, value_mat, preferred_element_type=jnp.float32
        ).astype(jnp.bfloat16)
        key_valid = key_positions[None, :] < (BLOCK * encoder_len[micro_idx])[:, None]
        query_valid = query_positions[None, :] < (BLOCK * decoder_len[micro_idx])[:, None]
        attended, grad_query, grad_key, grad_value = attend(
            queries[0, micro_idx].reshape(examples, dec_rows, heads_dev, HD),
            key_rows.reshape(examples, enc_rows, heads_dev, HD),
            value_rows.reshape(examples, enc_rows, heads_dev, HD),
            cotangent[0, micro_idx].reshape(examples, dec_rows, heads_dev, HD),
            key_valid,
            query_valid,
        )
        key_flat = grad_key.reshape(examples, enc_rows, width_dev)
        value_flat = grad_value.reshape(examples, enc_rows, width_dev)
        key_acc = key_acc + jnp.einsum(
            "ekd,ekc->dc", whole_enc, key_flat, preferred_element_type=jnp.float32
        )
        value_acc = value_acc + jnp.einsum(
            "ekd,ekc->dc", whole_enc, value_flat, preferred_element_type=jnp.float32
        )
        sections = lax.axis_size("section")
        key_blocks = key_mat.reshape(sections, key_mat.shape[0] // sections, width_dev)
        value_blocks = value_mat.reshape(sections, value_mat.shape[0] // sections, width_dev)
        feature_blocks = (
            jnp.einsum("ekc,fdc->fked", key_flat, key_blocks, preferred_element_type=jnp.float32)
            + jnp.einsum(
                "ekc,fdc->fked", value_flat, value_blocks, preferred_element_type=jnp.float32
            )
        ).astype(jnp.bfloat16)
        from_sections = lax.all_to_all(feature_blocks, "section", 0, 0, tiled=True)
        encoder_list.append(jnp.sum(from_sections.astype(jnp.float32), axis=0))
        attn_list.append(attended.reshape(examples, dec_rows, width_dev))
        query_list.append(grad_query.reshape(examples, dec_rows, width_dev))
    attention = jnp.stack(attn_list)[None]
    query_grads = jnp.stack(query_list)[None]
    key_grads = key_acc.astype(jnp.bfloat16)[None]
    value_grads = value_acc.astype(jnp.bfloat16)[None]
    section_share = jnp.stack(encoder_list)
    micro, enc_rows_all, examples_all, width_sec = section_share.shape
    row_blocks = section_share.reshape(
        micro, groups, enc_rows_all // groups, examples_all, width_sec
    ).transpose(1, 0, 3, 2, 4)
    received = lax.all_to_all(row_blocks, "dp", 0, 0, tiled=True)
    grad_encoder = jnp.sum(received, axis=0)
    return (attention, query_grads, key_grads, value_grads, grad_encoder)


def solution(mesh):
    placed = (
        P(None, None, "dp", "section"),
        P(),
        P(),
        P("section", None, None, None, "dp"),
        P("section", None, None, None, "dp"),
        P("section", None, "dp"),
        P("section", None, "dp"),
    )
    return jax.shard_map(
        body,
        mesh=mesh,
        in_specs=placed,
        out_specs=(
            P("section", None, None, None, "dp"),
            P("section", None, None, None, "dp"),
            P("section", None, "dp"),
            P("section", None, "dp"),
            P(None, None, "dp", "section"),
        ),
        check_vma=False,
    )
```

profile of v0, /device:TPU:32, one launch (start us, length us, event | category | flops | bytes accessed | tf_op | source)
XLA Modules:
  0.0 275.1 jit_solution(1751855742102394611)
XLA Ops:
  8.2 27.6 %all_to_all.20 = bf16[16,2,2,16,256]{4,3,2,1,0:T(8,128)(2,1)S(1)} all-to-all(bf16[16,2,2,16,256]{4,3,2,1,0:T(8,128)(2,1)S(1)} %broadcast_in_dim.88), channel_id=1, replica_groups=mesh['section'=16,'dp'=16] {'dp'}, dimensions={0} | all-to-all | bytes 1048576 | tf_op jit(solution)/shard_map/all_to_all | solution.py:62
  38.3 59.1 %all-gather.2.cloned.1.call-done = bf16[2,2,256,4096]{3,2,1,0:T(8,128)(2,1)} async-done(((bf16[2,2,256,256]{3,2,1,0:T(8,128)(2,1)}), bf16[2,2,256,4096]{3,2,1,0:T(8,128)(2,1)}) %all-gather.2.cloned.1.call-update) | async-done | bytes 8388624 | tf_op jit(solution)/shard_map/all_gather | solution.py:66
  97.4 4.2 %fusion.42 = bf16[2,256,256]{2,1,0:T(8,128)(2,1)S(1)} fusion(bf16[1,4096,256]{2,1,0:T(8,128)(2,1)} %param.13, bf16[2,2,256,4096]{3,2,1,0:T(8,128)(2,1)} %all-gather.2.cloned.1.call-done), kind=kOutput, calls=%fused_computation.52 | convolution fusion | flops 1073872896 | bytes 6553600 | tf_op jit(solution)/shard_map/ekd,dc->ekc/dot_general | solution.py:72
  105.3 1.6 convolution_convert_fusion.1
  106.9 2.1 convolution_convert_fusion.3
  110.6 1.3 fusion.10
  112.0 2.2 copy.81
  114.2 4.9 %all-to-all-start.1 = ((bf16[16,256,2,256]{3,1,2,0:T(8,128)(2,1)}), bf16[16,256,2,256]{3,1,2,0:T(8,128)(2,1)}, u32[]{:S(2)}, u32[]{:S(2)}) async-start(bf16[16,256,2,256]{3,1,2,0:T(8,128)(2,1)} %copy.81), calls=%async_computation.1 | async-start | bytes 8388608 | tf_op jit(solution)/shard_map/all_to_all | solution.py:102
  119.1 4.1 %fusion.36 = bf16[2,256,256]{2,1,0:T(8,128)(2,1)S(1)} fusion(bf16[1,4096,256]{2,1,0:T(8,128)(2,1)} %param.13, bf16[2,2,256,4096]{3,2,1,0:T(8,128)(2,1)} %all-gather.2.cloned.1.call-done), kind=kOutput, calls=%fused_computation.50 | convolution fusion | flops 1073872896 | bytes 6553600 | tf_op jit(solution)/shard_map/ekd,dc->ekc/dot_general | solution.py:72
  124.4 3.4 %fusion.39 = bf16[2,256,256]{2,1,0:T(8,128)(2,1)S(1)} fusion(bf16[1,4096,256]{2,1,0:T(8,128)(2,1)S(1)} %copy-done, bf16[2,2,256,4096]{3,2,1,0:T(8,128)(2,1)} %all-gather.2.cloned.1.call-done), kind=kOutput, calls=%fused_computation.51 | convolution fusion | flops 1073872896 | bytes 6553600 | tf_op jit(solution)/shard_map/ekd,dc->ekc/dot_general | solution.py:69
  127.8 2.2 fusion.126
  130.0 2.0 convolution_convert_fusion.2
  132.0 1.8 convolution_convert_fusion
  133.8 1.3 fusion.66
  135.4 1.3 fusion.11
  136.7 2.2 copy.84
  139.0 29.4 %all-to-all-done.1 = bf16[16,256,2,256]{3,1,2,0:T(8,128)(2,1)} async-done(((bf16[16,256,2,256]{3,1,2,0:T(8,128)(2,1)}), bf16[16,256,2,256]{3,1,2,0:T(8,128)(2,1)}, u32[]{:S(2)}, u32[]{:S(2)}) %all-to-all-start.1) | async-done | bytes 4194336 | tf_op jit(solution)/shard_map/all_to_all | solution.py:102
  168.3 5.6 %all-to-all-start.2 = ((bf16[16,256,2,256]{3,1,2,0:T(8,128)(2,1)}), bf16[16,256,2,256]{3,1,2,0:T(8,128)(2,1)}, u32[]{:S(2)}, u32[]{:S(2)}) async-start(bf16[16,256,2,256]{3,1,2,0:T(8,128)(2,1)} %copy.84), calls=%async_computation.2 | async-start | bytes 8388608 | tf_op jit(solution)/shard_map/all_to_all | solution.py:102
  176.3 2.1 fusion.52
  178.3 2.6 fusion.53
  181.0 2.8 %convert_reduce_fusion.1 = f32[256,2,256]{2,0,1:T(8,128)S(1)} fusion(bf16[16,256,2,256]{3,1,2,0:T(8,128)(2,1)} %all-to-all-done.1), kind=kLoop, calls=%fused_computation.6 | loop fusion | flops 4063232 | bytes 4718592 | tf_op jit(solution)/shard_map/reduce_sum | solution.py:103
  184.2 39.0 %all-to-all-done.2 = bf16[16,256,2,256]{3,1,2,0:T(8,128)(2,1)} async-done(((bf16[16,256,2,256]{3,1,2,0:T(8,128)(2,1)}), bf16[16,256,2,256]{3,1,2,0:T(8,128)(2,1)}, u32[]{:S(2)}, u32[]{:S(2)}) %all-to-all-start.2) | async-done | bytes 4194336 | tf_op jit(solution)/shard_map/all_to_all | solution.py:102
  223.2 2.8 %convert_reduce_fusion = f32[256,2,256]{2,0,1:T(8,128)S(1)} fusion(bf16[16,256,2,256]{3,1,2,0:T(8,128)(2,1)} %all-to-all-done.2), kind=kLoop, calls=%fused_computation.4 | loop fusion | flops 4063232 | bytes 4718592 | tf_op jit(solution)/shard_map/reduce_sum | solution.py:103
  226.4 1.8 maximum_bitcast_fusion
  228.3 8.2 %all-to-all-start.3 = ((f32[16,2,2,16,256]{4,2,3,1,0:T(2,128)}), f32[16,2,2,16,256]{4,2,3,1,0:T(2,128)S(1)}, u32[]{:S(2)}, u32[]{:S(2)}) async-start(f32[16,2,2,16,256]{4,2,3,1,0:T(2,128)} %maximum_bitcast_fusion), calls=%async_computation.3 | async-start | bytes 2097152 | tf_op jit(solution)/shard_map/all_to_all | solution.py:115
  238.5 3.6 %convolution_bitcast_fusion.2 = f32[256,4096]{1,0:T(8,128)S(1)} fusion(bf16[2,256,256]{2,1,0:T(8,128)(2,1)S(1)} %copy-done.8, bf16[2,2,256,4096]{3,2,1,0:T(8,128)(2,1)} %all-gather.2.cloned.1.call-done), kind=kOutput, calls=%fused_computation.10 | convolution fusion | flops 1073741824 | bytes 8650752 | tf_op jit(solution)/shard_map/ekd,ekc->dc/dot_general | solution.py:87
  242.0 3.6 %fusion.8 = bf16[1,4096,256]{1,2,0:T(8,128)(2,1)S(1)} fusion(f32[256,4096]{1,0:T(8,128)S(1)} %convolution_bitcast_fusion.2, bf16[2,256,256]{2,1,0:T(8,128)(2,1)S(1)} %copy-done.10, bf16[2,2,256,4096]{3,2,1,0:T(8,128)(2,1)} %all-gather.2.cloned.1.call-done), kind=kOutput, calls=%fused_computation.16 | convolution fusion | flops 1075838976 | bytes 10747904 | tf_op jit(solution)/shard_map/ekd,ekc->dc/dot_general | solution.py:87
  245.7 2.5 copy.90
  248.1 3.5 %convolution_bitcast_fusion = f32[256,4096]{1,0:T(8,128)S(1)} fusion(bf16[2,2,256,4096]{3,2,1,0:T(8,128)(2,1)} %all-gather.2.cloned.1.call-done, bf16[2,256,256]{2,1,0:T(8,128)(2,1)S(1)} %convolution_convert_fusion), kind=kOutput, calls=%fused_computation.8 | convolution fusion | flops 1073741824 | bytes 8650752 | tf_op jit(solution)/shard_map/ekd,ekc->dc/dot_general | solution.py:90
  251.6 5.1 %fusion.9 = bf16[1,4096,256]{1,2,0:T(8,128)(2,1)} fusion(f32[256,4096]{1,0:T(8,128)S(1)} %convolution_bitcast_fusion, bf16[2,2,256,4096]{3,2,1,0:T(8,128)(2,1)} %all-gather.2.cloned.1.call-done, bf16[2,256,256]{2,1,0:T(8,128)(2,1)S(1)} %copy-done.6), kind=kOutput, calls=%fused_computation.17 | convolution fusion | flops 1075838976 | bytes 10747904 | tf_op jit(solution)/shard_map/ekd,ekc->dc/dot_general | solution.py:90
  256.7 4.1 %copy.91 = bf16[1,4096,256]{2,1,0:T(8,128)(2,1)} copy(bf16[1,4096,256]{1,2,0:T(8,128)(2,1)} %fusion.9) | data formatting | bytes 4194304
  260.8 6.4 %all-to-all-done.3 = f32[16,2,2,16,256]{4,2,3,1,0:T(2,128)S(1)} async-done(((f32[16,2,2,16,256]{4,2,3,1,0:T(2,128)}), f32[16,2,2,16,256]{4,2,3,1,0:T(2,128)S(1)}, u32[]{:S(2)}, u32[]{:S(2)}) %all-to-all-start.3) | async-done | bytes 1048608 | tf_op jit(solution)/shard_map/all_to_all | solution.py:115
  (63 shorter events, 16.3 us)
Async XLA Ops:
  7.2 95.6 %copy-start = (bf16[1,4096,256]{2,1,0:T(8,128)(2,1)S(1)}, bf16[1,4096,256]{2,1,0:T(8,128)(2,1)}, u32[]{:S(2)}) copy-start(bf16[1,4096,256]{2,1,0:T(8,128)(2,1)} %param.12) | copy-start | bytes 6291460
  7.2 90.2 %all-gather.2.cloned.1.call-start = ((), (), s32[]{:S(2)}) async-start(), calls=%async_computation.4 | async-start | bytes 8912896 | tf_op jit(solution)/shard_map/all_gather | solution.py:66
  38.3 63.4 %copy-start.11 = (bf16[1,2,2,256,256]{4,3,2,1,0:T(8,128)(2,1)S(1)}, bf16[1,2,2,256,256]{4,3,2,1,0:T(8,128)(2,1)}, u32[]{:S(2)}) copy-start(bf16[1,2,2,256,256]{4,3,2,1,0:T(8,128)(2,1)} %param.11) | copy-start | bytes 1572868
  97.4 5.4 %copy-start.2 = (bf16[2,2,256,4096]{3,2,1,0:T(8,128)(2,1)S(1)}, bf16[2,2,256,4096]{3,2,1,0:T(8,128)(2,1)}, u32[]{:S(2)}) copy-start(bf16[2,2,256,4096]{3,2,1,0:T(8,128)(2,1)} %all-gather.2.cloned.1.call-done) | copy-start | bytes 25165828
  101.6 2.5 copy-start.12
  102.8 1.3 copy-start.14
  104.1 6.2 %copy-start.16 = (bf16[2,256,256]{2,1,0:T(8,128)(2,1)}, bf16[2,256,256]{2,1,0:T(8,128)(2,1)S(1)}, u32[]{:S(2)}) copy-start(bf16[2,256,256]{2,1,0:T(8,128)(2,1)S(1)} %fusion.45) | copy-start | bytes 786436
  106.9 3.4 %copy-start.5 = (bf16[2,256,256]{2,1,0:T(8,128)(2,1)}, bf16[2,256,256]{2,1,0:T(8,128)(2,1)S(1)}, u32[]{:S(2)}) copy-start(bf16[2,256,256]{2,1,0:T(8,128)(2,1)S(1)} %convolution_convert_fusion.1) | copy-start | bytes 786436
  108.9 1.3 copy-start.9
  109.0 1.7 copy-start.3
  114.2 54.2 %all-to-all-start.1 = ((bf16[16,256,2,256]{3,1,2,0:T(8,128)(2,1)}), bf16[16,256,2,256]{3,1,2,0:T(8,128)(2,1)}, u32[]{:S(2)}, u32[]{:S(2)}) async-start(bf16[16,256,2,256]{3,1,2,0:T(8,128)(2,1)} %copy.81), calls=%async_computation.1 | async-start | bytes 8388608 | tf_op jit(solution)/shard_map/all_to_all | solution.py:102
  127.8 2.2 copy-start.18
  132.0 3.1 %copy-start.7 = (bf16[2,256,256]{2,1,0:T(8,128)(2,1)}, bf16[2,256,256]{2,1,0:T(8,128)(2,1)S(1)}, u32[]{:S(2)}) copy-start(bf16[2,256,256]{2,1,0:T(8,128)(2,1)S(1)} %convolution_convert_fusion.2) | copy-start | bytes 786436
  133.8 1.6 copy-start.4
  138.9 35.0 %copy-start.13 = (bf16[2,256,256]{2,1,0:T(8,128)(2,1)S(1)}, bf16[2,256,256]{2,1,0:T(8,128)(2,1)}, u32[]{:S(2)}) copy-start(bf16[2,256,256]{2,1,0:T(8,128)(2,1)} %copy-done.12) | copy-start | bytes 786436
  139.0 35.0 %copy-start.15 = (bf16[1,2,2,256,256]{4,3,2,1,0:T(8,128)(2,1)S(1)}, bf16[1,2,2,256,256]{4,3,2,1,0:T(8,128)(2,1)}, u32[]{:S(2)}) copy-start(bf16[1,2,2,256,256]{4,3,2,1,0:T(8,128)(2,1)} %param.10) | copy-start | bytes 1572868
  139.0 35.0 %copy-start.17 = (bf16[2,256,256]{2,1,0:T(8,128)(2,1)S(1)}, bf16[2,256,256]{2,1,0:T(8,128)(2,1)}, u32[]{:S(2)}) copy-start(bf16[2,256,256]{2,1,0:T(8,128)(2,1)} %copy-done.16) | copy-start | bytes 786436
  139.0 35.6 %copy-start.19 = (bf16[2,256,256]{2,1,0:T(8,128)(2,1)S(1)}, bf16[2,256,256]{2,1,0:T(8,128)(2,1)}, u32[]{:S(2)}) copy-start(bf16[2,256,256]{2,1,0:T(8,128)(2,1)} %copy-done.18) | copy-start | bytes 786436
  168.3 54.8 %all-to-all-start.2 = ((bf16[16,256,2,256]{3,1,2,0:T(8,128)(2,1)}), bf16[16,256,2,256]{3,1,2,0:T(8,128)(2,1)}, u32[]{:S(2)}, u32[]{:S(2)}) async-start(bf16[16,256,2,256]{3,1,2,0:T(8,128)(2,1)} %copy.84), calls=%async_computation.2 | async-start | bytes 8388608 | tf_op jit(solution)/shard_map/all_to_all | solution.py:102
  226.0 12.4 %copy-start.8 = (bf16[2,256,256]{2,1,0:T(8,128)(2,1)S(1)}, bf16[2,256,256]{2,1,0:T(8,128)(2,1)}, u32[]{:S(2)}) copy-start(bf16[2,256,256]{2,1,0:T(8,128)(2,1)} %copy-done.7) | copy-start | bytes 786436
  228.3 38.9 %all-to-all-start.3 = ((f32[16,2,2,16,256]{4,2,3,1,0:T(2,128)}), f32[16,2,2,16,256]{4,2,3,1,0:T(2,128)S(1)}, u32[]{:S(2)}, u32[]{:S(2)}) async-start(f32[16,2,2,16,256]{4,2,3,1,0:T(2,128)} %maximum_bitcast_fusion), calls=%async_computation.3 | async-start | bytes 2097152 | tf_op jit(solution)/shard_map/all_to_all | solution.py:115
  238.5 3.6 %copy-start.10 = (bf16[2,256,256]{2,1,0:T(8,128)(2,1)S(1)}, bf16[2,256,256]{2,1,0:T(8,128)(2,1)}, u32[]{:S(2)}) copy-start(bf16[2,256,256]{2,1,0:T(8,128)(2,1)} %copy-done.9) | copy-start | bytes 786436
  248.1 3.5 %copy-start.6 = (bf16[2,256,256]{2,1,0:T(8,128)(2,1)S(1)}, bf16[2,256,256]{2,1,0:T(8,128)(2,1)}, u32[]{:S(2)}) copy-start(bf16[2,256,256]{2,1,0:T(8,128)(2,1)} %copy-done.5) | copy-start | bytes 786436
  251.6 16.6 %copy-start.1 = (bf16[1,4096,256]{2,1,0:T(8,128)(2,1)S(1)}, bf16[1,4096,256]{2,1,0:T(8,128)(2,1)}, u32[]{:S(2)}) copy-start(bf16[1,4096,256]{2,1,0:T(8,128)(2,1)} %param.12) | copy-start | bytes 6291460
Sparse Core Ops, SparseCore 0:
  36.7 60.6 all-gather.1
where the time goes:
time: 276 us; the launch traced here: 275 us
  waiting for transfers between devices  134 us (49%)
  matrix products  52.9 us (19%)
  blocking collectives  27.6 us (10%)
  starting transfers between devices  18.8 us (7%)
  local copies, waits for them, and re-layouts  16.9 us (6%)
  between operations  14.4 us (5%)
  other arithmetic  10.6 us (4%)
    all_to_all x2, waiting for transfers between devices, body(): from_sections = lax.all_to_all(feature_blocks, 'section', 0, 0, tiled=True)  68.4 us
    all_gather x1, waiting for transfers between devices, body(): gathered_enc = lax.all_gather(tall_enc, 'section', axis=3, tiled=True)  59.1 us
    all_to_all x1, blocking collectives, body(): from_each = lax.all_to_all(copies, 'dp', 0, 0, tiled=True)  27.6 us
    all_to_all x2, starting transfers between devices, body(): from_sections = lax.all_to_all(feature_blocks, 'section', 0, 0, tiled=True)  10.6 us
    unnamed x45, local copies, waits for them, and re-layouts  9.88 us
    dot_general x2, matrix products, body(): jnp.einsum('ekd,ekc->dc', whole_enc, value_flat, preferred_element_type=j...  8.57 us
    dot_general x2, matrix products, body(): jnp.einsum('ekd,dc->ekc', whole_enc, value_mat, preferred_element_type=jn...  8.36 us
    all_to_all x1, starting transfers between devices, body(): received = lax.all_to_all(row_blocks, 'dp', 0, 0, tiled=True)  8.18 us
  transfers between devices with their start and end apart: 4, of which 4 were waited for; matrix products, arithmetic and copies ran while one was open for 20% of the time, Pallas kernels for 0%

commit v1 on v0

--- a/solution.py
+++ b/solution.py
@@ -63,7 +63,15 @@
     tall_enc = jnp.moveaxis(from_each, 0, 2).reshape(
         encoder_out.shape[:2] + (groups * encoder_out.shape[2], encoder_out.shape[3])
     )
-    gathered_enc = lax.all_gather(tall_enc, "section", axis=3, tiled=True)
+    gathered_enc = jnp.concatenate(
+        lax.all_to_all(
+            jnp.stack(lax.axis_size("section") * [tall_enc], axis=0),
+            axis_name="section",
+            split_axis=0,
+            concat_axis=0,
+        ),
+        axis=3,
+    )
     for micro_idx in range(MICRO):
         whole_enc = gathered_enc[micro_idx]
         key_rows = jnp.einsum(

time: 276 us -> 320 us (1.16)
  local copies, waits for them, and re-layouts: 16.9 us -> 56.2 us
  waiting for transfers between devices: 134 us -> 149 us
  between operations: 14.4 us -> 0.96 us
    all_to_all x0 -> x1, waiting for transfers between devices: none -> 93.9 us  [body(): lax.all_to_all(jnp.stack(lax.axis_size('section') * [tall_enc], axis=0),...]
    all_gather x1 -> x0, waiting for transfers between devices: 59.1 us -> none  [body(): gathered_enc = lax.all_gather(tall_enc, 'section', axis=3, tiled=True)]
    slice x0 -> x3, local copies, waits for them, and re-layouts: none -> 16.1 us  [body(): whole_enc = gathered_enc[micro_idx]]
    all_to_all x2, waiting for transfers between devices: 68.4 us -> 53.1 us  [body(): from_sections = lax.all_to_all(feature_blocks, 'section', 0, 0, tiled=True)]
    squeeze x0 -> x2, local copies, waits for them, and re-layouts: none -> 14.8 us  [body(): whole_enc = gathered_enc[micro_idx]]
    all_to_all x0 -> x1, starting transfers between devices: none -> 5.91 us  [body(): lax.all_to_all(jnp.stack(lax.axis_size('section') * [tall_enc], axis=0),...]
    unnamed x45 -> x49, local copies, waits for them, and re-layouts: 9.88 us -> 14.8 us
    another operation x0 -> x1, local copies, waits for them, and re-layouts: none -> 4.22 us  [body(): jnp.stack(lax.axis_size('section') * [tall_enc], axis=0)]
  transfers between devices with their start and end apart: 4 -> 4, of which waited for: 4 -> 4; matrix products, arithmetic and copies ran while one was open for 20% -> 23% of each run, Pallas kernels for 0% -> 0%
where the time goes in v1:
time: 320 us; the launch traced here: 319 us
  waiting for transfers between devices  149 us (47%)
  local copies, waits for them, and re-layouts  56.2 us (18%)
  matrix products  51.6 us (16%)
  blocking collectives  27.6 us (9%)
  starting transfers between devices  21.8 us (7%)
  other arithmetic  11.6 us (4%)
    all_to_all x1, waiting for transfers between devices, body(): lax.all_to_all(jnp.stack(lax.axis_size('section') * [tall_enc], axis=0),...  93.9 us
    all_to_all x2, waiting for transfers between devices, body(): from_sections = lax.all_to_all(feature_blocks, 'section', 0, 0, tiled=True)  53.1 us
    all_to_all x1, blocking collectives, body(): from_each = lax.all_to_all(copies, 'dp', 0, 0, tiled=True)  27.6 us
    slice x3, local copies, waits for them, and re-layouts, body(): whole_enc = gathered_enc[micro_idx]  16.1 us
    unnamed x49, local copies, waits for them, and re-layouts  14.8 us
    squeeze x2, local copies, waits for them, and re-layouts, body(): whole_enc = gathered_enc[micro_idx]  14.8 us
    all_to_all x2, starting transfers between devices, body(): from_sections = lax.all_to_all(feature_blocks, 'section', 0, 0, tiled=True)  11.2 us
  transfers between devices with their start and end apart: 4, of which 4 were waited for; matrix products, arithmetic and copies ran while one was open for 23% of the time, Pallas kernels for 0%

profile of v1, /device:TPU:32, one launch (start us, length us, event | category | flops | bytes accessed | tf_op | source)
XLA Modules:
  0.0 318.9 jit_solution(12827776979003886267)
XLA Ops:
  1.6 27.6 %all_to_all.25 = bf16[16,2,2,16,256]{4,3,2,1,0:T(8,128)(2,1)S(1)} all-to-all(bf16[16,2,2,16,256]{4,3,2,1,0:T(8,128)(2,1)S(1)} %broadcast_in_dim.88), channel_id=1, replica_groups=mesh['section'=16,'dp'=16] {'dp'}, dimensions={0} | all-to-all | bytes 1048576 | tf_op jit(solution)/shard_map/all_to_all | solution.py:62
  29.2 4.2 %stack.18 = bf16[16,2,2,256,256]{4,3,2,1,0:T(8,128)(2,1)} broadcast(bf16[2,2,256,256]{3,2,1,0:T(8,128)(2,1)S(1)} %bitcast.254), dimensions={1,2,3,4} | broadcast | bytes 8912896 | tf_op jit(solution)/shard_map/stack | solution.py:68
  33.4 5.9 %all-to-all-start.1 = ((bf16[16,2,2,256,256]{4,3,2,1,0:T(8,128)(2,1)}), bf16[16,2,2,256,256]{4,3,2,1,0:T(8,128)(2,1)}, u32[]{:S(2)}, u32[]{:S(2)}) async-start(bf16[16,2,2,256,256]{4,3,2,1,0:T(8,128)(2,1)} %stack.18), calls=%async_computation.1 | async-start | bytes 16777216 | tf_op jit(solution)/shard_map/all_to_all | solution.py:67
  39.5 93.9 %all-to-all-done.1 = bf16[16,2,2,256,256]{4,3,2,1,0:T(8,128)(2,1)} async-done(((bf16[16,2,2,256,256]{4,3,2,1,0:T(8,128)(2,1)}), bf16[16,2,2,256,256]{4,3,2,1,0:T(8,128)(2,1)}, u32[]{:S(2)}, u32[]{:S(2)}) %all-to-all-start.1) | async-done | bytes 8388640 | tf_op jit(solution)/shard_map/all_to_all | solution.py:67
  133.5 5.1 %fusion.126 = (bf16[1,2,256,16,256]{4,2,1,0,3:T(8,128)(2,1)S(1)}, bf16[1,2,256,16,256]{4,2,1,0,3:T(8,128)(2,1)}) fusion(bf16[2,2,256,16,256]{4,2,1,0,3:T(8,128)(2,1)} %bitcast.3), kind=kLoop, calls=%fused_computation.129 | loop fusion | bytes 16777216 | tf_op jit(solution)/shard_map/slice | solution.py:76
  138.6 4.4 %copy.96 = bf16[1,2,256,16,256]{4,3,2,1,0:T(8,128)(2,1)} copy(bf16[1,2,256,16,256]{4,2,1,0,3:T(8,128)(2,1)S(1)} %get-tuple-element.25) | data formatting | bytes 8388608 | tf_op jit(solution)/shard_map/slice | solution.py:76
  143.0 7.4 %squeeze.16 = bf16[2,256,4096]{2,1,0:T(8,128)(2,1)} reshape(bf16[1,2,256,16,256]{4,3,2,1,0:T(8,128)(2,1)} %copy.96) | data formatting | bytes 8388608 | tf_op jit(solution)/shard_map/squeeze | solution.py:76
  150.4 3.6 %fusion.42 = bf16[2,256,256]{2,1,0:T(8,128)(2,1)S(1)} fusion(bf16[2,256,4096]{2,1,0:T(8,128)(2,1)} %squeeze.16, bf16[1,4096,256]{2,1,0:T(8,128)(2,1)S(1)} %copy-done), kind=kOutput, calls=%fused_computation.50 | convolution fusion | flops 1073872896 | bytes 6553600 | tf_op jit(solution)/shard_map/ekd,dc->ekc/dot_general | solution.py:77
  160.4 2.2 convolution_convert_fusion.3
  165.7 2.2 copy.115
  167.9 5.6 %all-to-all-start.2 = ((bf16[16,256,2,256]{3,1,2,0:T(8,128)(2,1)}), bf16[16,256,2,256]{3,1,2,0:T(8,128)(2,1)}, u32[]{:S(2)}, u32[]{:S(2)}) async-start(bf16[16,256,2,256]{3,1,2,0:T(8,128)(2,1)} %copy.115), calls=%async_computation.2 | async-start | bytes 8388608 | tf_op jit(solution)/shard_map/all_to_all | solution.py:110
  173.5 6.5 %copy.100 = bf16[1,2,256,16,256]{4,3,2,1,0:T(8,128)(2,1)} copy(bf16[1,2,256,16,256]{4,2,1,0,3:T(8,128)(2,1)} %get-tuple-element.26) | data formatting | bytes 8388608 | tf_op jit(solution)/shard_map/slice | solution.py:76
  180.0 7.4 %squeeze.19 = bf16[2,256,4096]{2,1,0:T(8,128)(2,1)} reshape(bf16[1,2,256,16,256]{4,3,2,1,0:T(8,128)(2,1)} %copy.100) | data formatting | bytes 8388608 | tf_op jit(solution)/shard_map/squeeze | solution.py:76
  187.4 4.2 %fusion.39 = bf16[2,256,256]{2,1,0:T(8,128)(2,1)S(1)} fusion(bf16[2,256,4096]{2,1,0:T(8,128)(2,1)} %squeeze.19, bf16[1,4096,256]{2,1,0:T(8,128)(2,1)} %param.13), kind=kOutput, calls=%fused_computation.49 | convolution fusion | flops 1073872896 | bytes 6553600 | tf_op jit(solution)/shard_map/ekd,dc->ekc/dot_general | solution.py:80
  194.1 2.2 fusion.127
  203.1 2.2 copy.118
  205.3 17.4 %all-to-all-done.2 = bf16[16,256,2,256]{3,1,2,0:T(8,128)(2,1)} async-done(((bf16[16,256,2,256]{3,1,2,0:T(8,128)(2,1)}), bf16[16,256,2,256]{3,1,2,0:T(8,128)(2,1)}, u32[]{:S(2)}, u32[]{:S(2)}) %all-to-all-start.2) | async-done | bytes 4194336 | tf_op jit(solution)/shard_map/all_to_all | solution.py:110
  222.7 5.6 %all-to-all-start.3 = ((bf16[16,256,2,256]{3,1,2,0:T(8,128)(2,1)}), bf16[16,256,2,256]{3,1,2,0:T(8,128)(2,1)}, u32[]{:S(2)}, u32[]{:S(2)}) async-start(bf16[16,256,2,256]{3,1,2,0:T(8,128)(2,1)} %copy.118), calls=%async_computation.3 | async-start | bytes 8388608 | tf_op jit(solution)/shard_map/all_to_all | solution.py:110
  228.4 3.0 fusion.52
  231.4 2.8 fusion.53
  234.2 2.3 fusion.55
  236.4 2.2 fusion.54
  238.7 2.8 convert_reduce_fusion.1
  241.9 35.7 %all-to-all-done.3 = bf16[16,256,2,256]{3,1,2,0:T(8,128)(2,1)} async-done(((bf16[16,256,2,256]{3,1,2,0:T(8,128)(2,1)}), bf16[16,256,2,256]{3,1,2,0:T(8,128)(2,1)}, u32[]{:S(2)}, u32[]{:S(2)}) %all-to-all-start.3) | async-done | bytes 4194336 | tf_op jit(solution)/shard_map/all_to_all | solution.py:110
  277.6 2.8 convert_reduce_fusion
  282.4 4.7 %all-to-all-start.4 = ((f32[16,2,2,16,256]{4,2,3,1,0:T(2,128)}), f32[16,2,2,16,256]{4,2,3,1,0:T(2,128)S(1)}, u32[]{:S(2)}, u32[]{:S(2)}) async-start(f32[16,2,2,16,256]{4,2,3,1,0:T(2,128)} %maximum_bitcast_fusion), calls=%async_computation.4 | async-start | bytes 2097152 | tf_op jit(solution)/shard_map/all_to_all | solution.py:123
  295.0 3.7 %convolution_bitcast_fusion.2 = f32[256,4096]{1,0:T(8,128)S(1)} fusion(bf16[2,256,256]{2,1,0:T(8,128)(2,1)} %copy-done.10, bf16[2,256,4096]{2,1,0:T(8,128)(2,1)} %squeeze.19), kind=kOutput, calls=%fused_computation.10 | convolution fusion | flops 1073741824 | bytes 8650752 | tf_op jit(solution)/shard_map/ekd,ekc->dc/dot_general | solution.py:95
  298.7 2.6 fusion.8
  301.3 4.1 %copy.124 = bf16[1,4096,256]{2,1,0:T(8,128)(2,1)} copy(bf16[1,4096,256]{1,2,0:T(8,128)(2,1)} %fusion.8) | data formatting | bytes 4194304
  305.4 3.6 %convolution_bitcast_fusion = f32[256,4096]{1,0:T(8,128)S(1)} fusion(bf16[2,256,4096]{2,1,0:T(8,128)(2,1)} %squeeze.19, bf16[2,256,256]{2,1,0:T(8,128)(2,1)S(1)} %convolution_convert_fusion), kind=kOutput, calls=%fused_computation.8 | convolution fusion | flops 1073741824 | bytes 8650752 | tf_op jit(solution)/shard_map/ekd,ekc->dc/dot_general | solution.py:98
  309.0 2.6 fusion.9
  311.6 4.1 %copy.125 = bf16[1,4096,256]{2,1,0:T(8,128)(2,1)} copy(bf16[1,4096,256]{1,2,0:T(8,128)(2,1)} %fusion.9) | data formatting | bytes 4194304
  (72 shorter events, 33.2 us)
Async XLA Ops:
  0.6 149.8 %copy-start = (bf16[1,4096,256]{2,1,0:T(8,128)(2,1)S(1)}, bf16[1,4096,256]{2,1,0:T(8,128)(2,1)}, u32[]{:S(2)}) copy-start(bf16[1,4096,256]{2,1,0:T(8,128)(2,1)} %param.12) | copy-start | bytes 6291460
  33.4 5.9 %copy-start.16 = (s32[2,2]{1,0:T(2,128)S(1)}, s32[2,2]{1,0:T(2,128)}, u32[]{:S(2)}) copy-start(s32[2,2]{1,0:T(2,128)} %param.8) | copy-start | bytes 52
  33.4 5.9 %copy-start.17 = (s32[2,2]{1,0:T(2,128)S(1)}, s32[2,2]{1,0:T(2,128)}, u32[]{:S(2)}) copy-start(s32[2,2]{1,0:T(2,128)} %param.9) | copy-start | bytes 52
  33.4 100.0 %all-to-all-start.1 = ((bf16[16,2,2,256,256]{4,3,2,1,0:T(8,128)(2,1)}), bf16[16,2,2,256,256]{4,3,2,1,0:T(8,128)(2,1)}, u32[]{:S(2)}, u32[]{:S(2)}) async-start(bf16[16,2,2,256,256]{4,3,2,1,0:T(8,128)(2,1)} %stack.18), calls=%async_computation.1 | async-start | bytes 16777216 | tf_op jit(solution)/shard_map/all_to_all | solution.py:67
  150.4 3.6 %copy-start.2 = (bf16[2,256,4096]{2,1,0:T(8,128)(2,1)S(1)}, bf16[2,256,4096]{2,1,0:T(8,128)(2,1)}, u32[]{:S(2)}) copy-start(bf16[2,256,4096]{2,1,0:T(8,128)(2,1)} %squeeze.16) | copy-start | bytes 12582916
  150.4 4.1 %copy-start.5 = (bf16[1,4096,256]{2,1,0:T(8,128)(2,1)S(1)}, bf16[1,4096,256]{2,1,0:T(8,128)(2,1)}, u32[]{:S(2)}) copy-start(bf16[1,4096,256]{2,1,0:T(8,128)(2,1)} %param.13) | copy-start | bytes 6291460
  154.5 4.3 %copy-start.20 = (bf16[2,256,256]{2,1,0:T(8,128)(2,1)}, bf16[2,256,256]{2,1,0:T(8,128)(2,1)S(1)}, u32[]{:S(2)}) copy-start(bf16[2,256,256]{2,1,0:T(8,128)(2,1)S(1)} %fusion.42) | copy-start | bytes 786436
  154.5 2.0 copy-start.13
  154.5 3.1 copy-start.18
  155.8 0.7 copy-start.14
  160.4 3.6 %copy-start.8 = (bf16[2,256,256]{2,1,0:T(8,128)(2,1)}, bf16[2,256,256]{2,1,0:T(8,128)(2,1)S(1)}, u32[]{:S(2)}) copy-start(bf16[2,256,256]{2,1,0:T(8,128)(2,1)S(1)} %convolution_convert_fusion.1) | copy-start | bytes 786436
  162.7 1.3 copy-start.11
  162.7 1.7 copy-start.6
  167.9 54.8 %all-to-all-start.2 = ((bf16[16,256,2,256]{3,1,2,0:T(8,128)(2,1)}), bf16[16,256,2,256]{3,1,2,0:T(8,128)(2,1)}, u32[]{:S(2)}, u32[]{:S(2)}) async-start(bf16[16,256,2,256]{3,1,2,0:T(8,128)(2,1)} %copy.115), calls=%async_computation.2 | async-start | bytes 8388608 | tf_op jit(solution)/shard_map/all_to_all | solution.py:110
  187.4 5.4 %copy-start.1 = (bf16[2,256,4096]{2,1,0:T(8,128)(2,1)S(1)}, bf16[2,256,4096]{2,1,0:T(8,128)(2,1)}, u32[]{:S(2)}) copy-start(bf16[2,256,4096]{2,1,0:T(8,128)(2,1)} %squeeze.19) | copy-start | bytes 12582916
  194.1 2.2 copy-start.21
  198.4 3.1 copy-start.10
  200.1 1.6 copy-start.7
  222.7 54.8 %all-to-all-start.3 = ((bf16[16,256,2,256]{3,1,2,0:T(8,128)(2,1)}), bf16[16,256,2,256]{3,1,2,0:T(8,128)(2,1)}, u32[]{:S(2)}, u32[]{:S(2)}) async-start(bf16[16,256,2,256]{3,1,2,0:T(8,128)(2,1)} %copy.118), calls=%async_computation.3 | async-start | bytes 8388608 | tf_op jit(solution)/shard_map/all_to_all | solution.py:110
  228.3 5.8 %copy-start.15 = (bf16[2,256,256]{2,1,0:T(8,128)(2,1)S(1)}, bf16[2,256,256]{2,1,0:T(8,128)(2,1)}, u32[]{:S(2)}) copy-start(bf16[2,256,256]{2,1,0:T(8,128)(2,1)} %copy-done.14) | copy-start | bytes 786436
  228.4 5.8 %copy-start.19 = (bf16[1,2,2,256,256]{4,3,2,1,0:T(8,128)(2,1)S(1)}, bf16[1,2,2,256,256]{4,3,2,1,0:T(8,128)(2,1)}, u32[]{:S(2)}) copy-start(bf16[1,2,2,256,256]{4,3,2,1,0:T(8,128)(2,1)} %param.10) | copy-start | bytes 1572868
  282.4 35.4 %all-to-all-start.4 = ((f32[16,2,2,16,256]{4,2,3,1,0:T(2,128)}), f32[16,2,2,16,256]{4,2,3,1,0:T(2,128)S(1)}, u32[]{:S(2)}, u32[]{:S(2)}) async-start(f32[16,2,2,16,256]{4,2,3,1,0:T(2,128)} %maximum_bitcast_fusion), calls=%async_computation.4 | async-start | bytes 2097152 | tf_op jit(solution)/shard_map/all_to_all | solution.py:123
  295.0 3.7 %copy-start.3 = (bf16[2,256,4096]{2,1,0:T(8,128)(2,1)S(1)}, bf16[2,256,4096]{2,1,0:T(8,128)(2,1)}, u32[]{:S(2)}) copy-start(bf16[2,256,4096]{2,1,0:T(8,128)(2,1)} %squeeze.16) | copy-start | bytes 12582916
  295.0 3.7 %copy-start.12 = (bf16[2,256,256]{2,1,0:T(8,128)(2,1)S(1)}, bf16[2,256,256]{2,1,0:T(8,128)(2,1)}, u32[]{:S(2)}) copy-start(bf16[2,256,256]{2,1,0:T(8,128)(2,1)} %copy-done.11) | copy-start | bytes 786436
  305.4 3.6 %copy-start.4 = (bf16[2,256,4096]{2,1,0:T(8,128)(2,1)S(1)}, bf16[2,256,4096]{2,1,0:T(8,128)(2,1)}, u32[]{:S(2)}) copy-start(bf16[2,256,4096]{2,1,0:T(8,128)(2,1)} %squeeze.16) | copy-start | bytes 12582916
  305.4 3.6 %copy-start.9 = (bf16[2,256,256]{2,1,0:T(8,128)(2,1)S(1)}, bf16[2,256,256]{2,1,0:T(8,128)(2,1)}, u32[]{:S(2)}) copy-start(bf16[2,256,256]{2,1,0:T(8,128)(2,1)} %copy-done.8) | copy-start | bytes 786436
